TPU v7x, 512 devices: a whole 4x8x8 slice. The times are simulated.
512 devices in a mesh: dp: 32 (over z, x), fsdp: 16 (over y, core).
Axes of the slice: x: 4, y: 8, z: 8, core: 2. Of those that a mesh axis runs over, the one named last changes fastest.
Arguments:
- projected: bfloat16 [65536, 2304], P(('dp', 'fsdp')), may hold values from -7.03125 to 7.03125
- out_weight: bfloat16 [768, 1536], P('fsdp'), may hold values from -0.21875 to 0.21875
- kernel: float32 [31, 1536], replicated, may hold values from -2 to 2
- cotangent: bfloat16 [65536, 1536], P(('dp', 'fsdp')), may hold values from -6 to 6
- send_rows: int32 [65536], P(('dp', 'fsdp')), may hold values from -1 to 127, as said below
- compute_src: int32 [65536], P(('dp', 'fsdp')), may hold values from -1 to 127, as said below
- segment: int32 [65536], P(('dp', 'fsdp')), may hold values from -1 to 3, as said below
Outputs:
- block_out: bfloat16 [65536, 1536], P(('dp', 'fsdp'))
- projected_grad: bfloat16 [65536, 2304], P(('dp', 'fsdp'))
- out_weight_grad: float32 [768, 1536], P('fsdp')
- kernel_grad: float32 [31, 1536], replicated
Inputs may be any that keep to these rules, and one draw needn't show every extreme that they name: `send_rows`: A device's 128 entries are 32 blocks of 4, block t for index t of dp at the same fsdp index; each lists rows of the device's own block of projected, each row at most once, filled entries first in a block and -1 after them. In every draw some device of each fsdp index fills all its entries. `compute_src`: on device (t, f), a row holds s * 4 + k when it receives entry t * 4 + k of device (s, f); every filled entry of send_rows is received by exactly one row, and a row holds -1 when it receives nothing. Filled rows come first. In every draw some device of each fsdp index receives a full block from every device. On each device, rows with compute_src = -1 hold -1, the others hold segment numbers from 0 that never fall along the rows.
All inputs are finite; a program needn't handle non-finite values.
Results may differ from a plain program's by a relative error of at most 0.018.
Values may be sent and summed in bfloat16 or wider, within the bound.
No kernel may reach another device: no remote copies, remote signals or barrier semaphores. Data moves between devices by JAX's collectives and lax.ppermute only.
A program may use at most 128 MiB of HBM per device.

v0:
```python
import jax
import jax.numpy as jnp
from jax import lax
from jax.sharding import PartitionSpec as P

HEADS = 8
HEAD_DIM = 96


def split_heads(frames):
    length = frames.shape[0]
    inner_width = HEADS * HEAD_DIM
    query_part = frames[:, :inner_width].reshape(length, HEADS, HEAD_DIM)
    key_part = frames[:, inner_width : 2 * inner_width].reshape(length, HEADS, HEAD_DIM)
    value_part = frames[:, 2 * inner_width :].reshape(length, HEADS, HEAD_DIM)
    return (query_part, key_part, value_part)


def attend(frames, segment):
    query_part, key_part, value_part = split_heads(frames)
    scores = jnp.einsum(
        "qhd,khd->hqk", query_part, key_part, preferred_element_type=jnp.float32
    ) * HEAD_DIM ** (-0.5)
    inside = segment[:, None] == segment[None, :]
    scores = jnp.where(inside[None], scores, -1e30)
    highest = jnp.max(scores, axis=2, keepdims=True)
    weights = jnp.exp(scores - highest)
    soft_probs = weights / jnp.sum(weights, axis=2, keepdims=True)
    rounded = soft_probs.astype(jnp.bfloat16)
    context = jnp.einsum("hqk,khd->qhd", rounded, value_part, preferred_element_type=jnp.float32)
    return (
        context.reshape(frames.shape[0], HEADS * HEAD_DIM).astype(jnp.bfloat16),
        soft_probs,
        rounded,
    )


def attend_back(frames, soft_probs, rounded, context_grad):
    query_part, key_part, value_part = split_heads(frames)
    length = frames.shape[0]
    inner_width = HEADS * HEAD_DIM
    upstream = context_grad.reshape(length, HEADS, HEAD_DIM)
    value_grad = jnp.einsum("hqk,qhd->khd", rounded, upstream, preferred_element_type=jnp.float32)
    prob_grad = jnp.einsum("qhd,khd->hqk", upstream, value_part, preferred_element_type=jnp.float32)
    score_grad = soft_probs * (prob_grad - jnp.sum(prob_grad * soft_probs, axis=2, keepdims=True))
    score_grad = (score_grad * HEAD_DIM ** (-0.5)).astype(jnp.bfloat16)
    query_grad = jnp.einsum(
        "hqk,khd->qhd", score_grad, key_part, preferred_element_type=jnp.float32
    )
    key_grad = jnp.einsum(
        "hqk,qhd->khd", score_grad, query_part, preferred_element_type=jnp.float32
    )
    return jnp.concatenate(
        [
            query_grad.reshape(length, inner_width).astype(jnp.bfloat16),
            key_grad.reshape(length, inner_width).astype(jnp.bfloat16),
            value_grad.reshape(length, inner_width).astype(jnp.bfloat16),
        ],
        axis=1,
    )


def finish(mixed, kernel, segment):
    length = mixed.shape[0]
    tap_count = kernel.shape[0]
    half_span = (tap_count - 1) // 2
    signal = mixed.astype(jnp.float32)
    padded = jnp.pad(signal, ((half_span, half_span), (0, 0)))
    neighbours = jnp.pad(segment, (half_span, half_span), constant_values=-2)
    convolved = jnp.zeros_like(signal)
    for offset in range(tap_count):
        matching = (neighbours[offset : offset + length] == segment).astype(jnp.float32)
        convolved = (
            convolved + kernel[offset] * padded[offset : offset + length] * matching[:, None]
        )
    return signal + jax.nn.silu(convolved)


def body(projected, out_weight, kernel, cotangent, send_rows, compute_src, segment):
    row_count = projected.shape[0]
    present = send_rows >= 0
    outgoing = jnp.take(projected, jnp.maximum(send_rows, 0), axis=0)
    outgoing = jnp.where(present[:, None], outgoing, jnp.zeros_like(outgoing))
    incoming = lax.all_to_all(outgoing, "dp", split_axis=0, concat_axis=0, tiled=True)
    filled = compute_src >= 0
    frames = jnp.take(incoming, jnp.maximum(compute_src, 0), axis=0)
    frames = jnp.where(filled[:, None], frames, jnp.zeros_like(frames))
    context, soft_probs, rounded = attend(frames, segment)
    columns = context
    mixed_sums = jnp.dot(
        columns,
        lax.all_gather(out_weight, "fsdp", axis=0, tiled=True),
        preferred_element_type=jnp.float32,
    )
    mixed = mixed_sums.astype(jnp.bfloat16)
    result, pullback = jax.vjp(
        lambda signal, kernel_taps: finish(signal, kernel_taps, segment), mixed, kernel
    )
    mixed_grad, kernel_part = pullback(cotangent.astype(jnp.float32))
    columns = context
    weight_share = lax.psum_scatter(
        jnp.einsum("rc,rd->cd", columns, mixed_grad, preferred_element_type=jnp.float32).astype(
            jnp.bfloat16
        ),
        "fsdp",
        scatter_dimension=0,
        tiled=True,
    ).astype(jnp.float32)
    context_grad = jnp.einsum(
        "rd,cd->rc",
        mixed_grad,
        lax.all_gather(out_weight, "fsdp", axis=0, tiled=True),
        preferred_element_type=jnp.float32,
    ).astype(jnp.bfloat16)
    frame_grad = attend_back(frames, soft_probs, rounded, context_grad)
    slot_total = incoming.shape[0]
    back_index = jnp.where(filled, compute_src, slot_total)
    returning = jnp.zeros_like(incoming).at[back_index].set(frame_grad, mode="drop")
    arrived = lax.all_to_all(returning, "dp", split_axis=0, concat_axis=0, tiled=True)
    source_index = jnp.where(present, send_rows, row_count)
    projected_grad = jnp.zeros_like(projected).at[source_index].set(arrived, mode="drop")
    scale_factor = (row_count * lax.axis_size("dp") * lax.axis_size("fsdp")) ** (-0.5)
    kernel_f = lax.psum(kernel_part, "fsdp")
    both = dp_allreduce_a2a(
        jnp.concatenate([weight_share, kernel_f, jnp.zeros((17, 1536), jnp.float32)], axis=0)
    )
    weight_total, kernel_total = (both[:48], both[48:79])
    return (
        result.astype(jnp.bfloat16),
        projected_grad,
        weight_total * scale_factor,
        kernel_total * scale_factor,
    )


def dp_allreduce_rs_ag(x):
    n = lax.axis_size("dp")
    flat = x.reshape(n, -1)
    part = lax.psum_scatter(flat, "dp", scatter_dimension=0, tiled=True)
    return lax.all_gather(part, "dp", axis=0, tiled=True).reshape(x.shape)


def dp_allreduce_a2a(x):
    n = lax.axis_size("dp")
    flat = x.reshape(n, -1)
    got = lax.all_to_all(flat, "dp", split_axis=0, concat_axis=0, tiled=True)
    part = jnp.sum(got, axis=0, keepdims=True)
    return lax.all_gather(part, "dp", axis=0, tiled=True).reshape(x.shape)


def dp_allreduce_a2a2(x):
    n = lax.axis_size("dp")
    flat = x.reshape(n, -1)
    got = lax.all_to_all(flat, "dp", split_axis=0, concat_axis=0, tiled=True)
    part = jnp.sum(got, axis=0, keepdims=True)
    back = lax.all_to_all(
        jnp.broadcast_to(part, flat.shape), "dp", split_axis=0, concat_axis=0, tiled=True
    )
    return back.reshape(x.shape)


def solution(mesh):
    placed = (
        P(("dp", "fsdp"), None),
        P("fsdp", None),
        P(),
        P(("dp", "fsdp"), None),
        P(("dp", "fsdp")),
        P(("dp", "fsdp")),
        P(("dp", "fsdp")),
    )
    return jax.shard_map(
        body,
        mesh=mesh,
        in_specs=placed,
        out_specs=(P(("dp", "fsdp"), None), P(("dp", "fsdp"), None), P("fsdp", None), P()),
        check_vma=False,
    )
```

profile of v0, /device:TPU:24, one launch (start us, length us, event | category | flops | bytes accessed | tf_op | source)
XLA Modules:
  0.0 341.6 jit_solution(10079741374050329405)
XLA Ops:
  7.2 0.7 all-gather.4.cloned.1.call-update
  7.9 1.2 compare_select_fusion.1
  9.1 1.0 gather_fusion
  10.2 0.2 select_select_fusion.1
  10.3 1.0 all_to_all.22
  11.3 13.2 %all-to-all-start = ((bf16[32,4,2304]{2,1,0:T(4,128)(2,1)}), bf16[32,4,2304]{2,1,0:T(4,128)(2,1)S(1)}, u32[]{:S(2)}, u32[]{:S(2)}) async-start(bf16[32,4,2304]{2,1,0:T(4,128)(2,1)} %all_to_all.22), calls=%async_computation | async-start | bytes 1179648 | tf_op jit(solution)/shard_map/all_to_all | solution.py:84
  24.5 0.2 slice_reduce_fusion.29
  24.7 0.5 compare_select_fusion
  25.3 0.3 slice_reduce_fusion.30
  26.0 17.5 %all-to-all-done = bf16[32,4,2304]{2,1,0:T(4,128)(2,1)S(1)} async-done(((bf16[32,4,2304]{2,1,0:T(4,128)(2,1)}), bf16[32,4,2304]{2,1,0:T(4,128)(2,1)S(1)}, u32[]{:S(2)}, u32[]{:S(2)}) %all-to-all-start) | async-done | bytes 589856 | tf_op jit(solution)/shard_map/all_to_all | solution.py:84
  43.6 1.0 gather_fusion.1
  44.6 0.2 select_select_fusion
  44.8 0.2 copy.36
  44.9 0.2 copy.35
  45.1 0.2 copy.34
  45.3 1.2 fusion.40
  46.4 0.5 convolution_convert_fusion.6
  47.0 9.4 %all-gather.4.cloned.1.call-done = bf16[768,1536]{1,0:T(8,128)(2,1)} async-done(((bf16[48,1536]{1,0:T(8,128)(2,1)}), bf16[768,1536]{1,0:T(8,128)(2,1)}) %all-gather.4.cloned.1.call-update) | async-done | bytes 2359312 | tf_op jit(solution)/shard_map/all_gather | solution.py:92
  56.4 2.2 fusion.2
  58.6 7.6 %multiply_reduce_fusion.31 = (f32[1536]{0:T(1024)}, f32[1536]{0:T(1024)}, f32[1536]{0:T(1024)}, f32[1536]{0:T(1024)}, f32[1536]{0:T(1024)}, /*index=5*/f32[1536]...) fusion(f32[128,1536]{1,0:T(8,128)S(1)} %fusion.2, ...), kind=kLoop, calls=%fused_computation.99 | loop fusion | flops 25152000 | bytes 3013632 | tf_op jit(solution)/shard_map/transpose(jvp())/reduce_sum | solution.py:74
  66.2 2.3 multiply_reduce_fusion.16
  68.4 0.5 multiply_multiply_fusion.27
  69.0 0.7 multiply_multiply_fusion.29
  69.8 0.7 multiply_multiply_fusion.28
  70.5 2.6 multiply_reduce_fusion.4
  73.1 2.8 pad_add_fusion
  75.9 0.7 fusion.16
  76.7 2.1 convolution_convert_fusion
  78.8 0.6 reshape.271
  79.4 0.6 reshape.272
  80.0 0.6 reshape.273
  80.6 0.6 reshape.274
  81.2 0.6 reshape.275
  81.8 0.6 reshape.276
  82.4 0.6 reshape.277
  83.0 0.6 reshape.278
  83.6 0.6 reshape.279
  84.2 2.5 convolution_convert_fusion.5
  86.8 0.2 copy.38
  87.0 1.3 convolution_convert_fusion.2
  88.3 0.1 copy.44
  88.4 0.3 fusion.41
  88.7 1.7 convolution_convert_fusion.3
  90.4 0.1 copy.43
  90.6 2.3 convolution_convert_fusion.4
  92.8 1.1 copy.42
  93.9 1.8 scatter_custom_fusion
  95.8 1.0 all_to_all.25
  96.8 10.3 %all-to-all-start.1 = ((bf16[32,4,2304]{2,1,0:T(4,128)(2,1)}), bf16[32,4,2304]{2,1,0:T(4,128)(2,1)S(1)}, u32[]{:S(2)}, u32[]{:S(2)}) async-start(bf16[32,4,2304]{2,1,0:T(4,128)(2,1)} %all_to_all.25), calls=%async_computation.1 | async-start | bytes 1179648 | tf_op jit(solution)/shard_map/all_to_all | solution.py:119
  107.2 2.4 multiply_reduce_fusion.22
  110.1 1.0 pad_add_fusion.7
  111.2 26.3 %reduce-scatter.2.cloned.1.call-done = bf16[48,1536]{1,0:T(8,128)(2,1)} async-done(((bf16[768,1536]{1,0:T(8,128)(2,1)}), bf16[48,1536]{1,0:T(8,128)(2,1)}) %reduce-scatter.2.cloned.1.call-update) | async-done | bytes 147472 | tf_op jit(solution)/shard_map/reduce_scatter | solution.py:101
  137.5 0.9 convert_element_type.212
  138.4 112.9 %all-reduce.66.cloned.1.call-done = f32[31,1536]{1,0:T(8,128)} async-done(((f32[31,1536]{1,0:T(8,128)}), f32[31,1536]{1,0:T(8,128)}) %all-reduce.66.cloned.1.call-update) | async-done | bytes 190480 | tf_op jit(solution)/shard_map/psum | solution.py:123
  251.3 1.0 maximum_maximum_fusion
  252.3 1.5 all_to_all.30
  253.8 10.2 %all-to-all-start.2 = ((f32[32,1,4608]{2,1,0:T(1,128)}), f32[32,1,4608]{2,1,0:T(1,128)S(1)}, u32[]{:S(2)}, u32[]{:S(2)}) async-start(f32[32,1,4608]{2,1,0:T(1,128)} %all_to_all.30), calls=%async_computation.3 | async-start | bytes 1179648 | tf_op jit(solution)/shard_map/all_to_all | solution.py:146
  264.2 2.4 scatter_custom_fusion.1
  266.6 17.0 %all-to-all-done.2 = f32[32,1,4608]{2,1,0:T(1,128)S(1)} async-done(((f32[32,1,4608]{2,1,0:T(1,128)}), f32[32,1,4608]{2,1,0:T(1,128)S(1)}, u32[]{:S(2)}, u32[]{:S(2)}) %all-to-all-start.2) | async-done | bytes 589856 | tf_op jit(solution)/shard_map/all_to_all | solution.py:146
  283.6 0.3 reduce_sum.356
  283.9 48.8 %all-gather.1 = f32[32,1,4608]{2,1,0:T(1,128)S(1)} all-gather(f32[1,1,4608]{2,1,0:T(1,128)S(1)} %reshape.348), channel_id=2, replica_groups=mesh['dp'=32,'fsdp'=16] {'dp'}, dimensions={0}, use_global_device_ids=true | all-gather | bytes 608256 | tf_op jit(solution)/shard_map/all_gather | solution.py:148
  332.7 0.8 fusion.23
  333.6 0.7 reshape.346
  334.3 0.8 mul.1323
  (144 shorter events, 1.2 us)
Async XLA Ops:
  7.2 2.0 copy-start
  7.2 49.2 %all-gather.4.cloned.1.call-start = ((), (), s32[]{:S(2)}) async-start(), calls=%async_computation.4 | async-start | bytes 2506752 | tf_op jit(solution)/shard_map/all_gather | solution.py:92
  9.1 1.0 copy-start.47
  10.1 14.4 %copy-start.6 = (f32[31,1536]{1,0:T(8,128)S(1)}, f32[31,1536]{1,0:T(8,128)}, u32[]{:S(2)}) copy-start(f32[31,1536]{1,0:T(8,128)} %param.11) | copy-start | bytes 571396
  10.1 14.6 %copy-start.48 = (s32[128]{0:T(128)S(1)}, s32[128]{0:T(128)}, u32[]{:S(2)}) copy-start(s32[128]{0:T(128)} %param.14) | copy-start | bytes 1540
  10.1 15.5 %copy-start.46 = (s32[128]{0:T(128)S(1)}, s32[128]{0:T(128)}, u32[]{:S(2)}) copy-start(s32[128]{0:T(128)} %param.15) | copy-start | bytes 1540
  11.3 32.2 %all-to-all-start = ((bf16[32,4,2304]{2,1,0:T(4,128)(2,1)}), bf16[32,4,2304]{2,1,0:T(4,128)(2,1)S(1)}, u32[]{:S(2)}, u32[]{:S(2)}) async-start(bf16[32,4,2304]{2,1,0:T(4,128)(2,1)} %all_to_all.22), calls=%async_computation | async-start | bytes 1179648 | tf_op jit(solution)/shard_map/all_to_all | solution.py:84
  24.4 113.0 %reduce-scatter.2.cloned.1.call-start = ((), (), s32[]{:S(2)}) async-start(), calls=%async_computation.5 | async-start | bytes 2506752 | tf_op jit(solution)/shard_map/reduce_scatter | solution.py:101
  25.8 43.2 %copy-start.43 = (f32[128]{0:T(128)}, f32[128]{0:T(128)S(1)}, u32[]{:S(2)}) copy-start(f32[128]{0:T(128)S(1)} %get-tuple-element.120) | copy-start | bytes 1540
  25.8 43.2 %copy-start.44 = (f32[128]{0:T(128)}, f32[128]{0:T(128)S(1)}, u32[]{:S(2)}) copy-start(f32[128]{0:T(128)S(1)} %get-tuple-element.121) | copy-start | bytes 1540
  25.8 43.2 %copy-start.45 = (f32[128]{0:T(128)}, f32[128]{0:T(128)S(1)}, u32[]{:S(2)}) copy-start(f32[128]{0:T(128)S(1)} %get-tuple-element.122) | copy-start | bytes 1540
  25.8 43.9 %copy-start.37 = (f32[128]{0:T(128)}, f32[128]{0:T(128)S(1)}, u32[]{:S(2)}) copy-start(f32[128]{0:T(128)S(1)} %get-tuple-element.114) | copy-start | bytes 1540
  25.8 43.9 %copy-start.38 = (f32[128]{0:T(128)}, f32[128]{0:T(128)S(1)}, u32[]{:S(2)}) copy-start(f32[128]{0:T(128)S(1)} %get-tuple-element.115) | copy-start | bytes 1540
  25.8 43.9 %copy-start.39 = (f32[128]{0:T(128)}, f32[128]{0:T(128)S(1)}, u32[]{:S(2)}) copy-start(f32[128]{0:T(128)S(1)} %get-tuple-element.116) | copy-start | bytes 1540
  25.9 43.9 %copy-start.40 = (f32[128]{0:T(128)}, f32[128]{0:T(128)S(1)}, u32[]{:S(2)}) copy-start(f32[128]{0:T(128)S(1)} %get-tuple-element.117) | copy-start | bytes 1540
  25.9 43.9 %copy-start.41 = (f32[128]{0:T(128)}, f32[128]{0:T(128)S(1)}, u32[]{:S(2)}) copy-start(f32[128]{0:T(128)S(1)} %get-tuple-element.118) | copy-start | bytes 1540
  25.9 43.9 %copy-start.42 = (f32[128]{0:T(128)}, f32[128]{0:T(128)S(1)}, u32[]{:S(2)}) copy-start(f32[128]{0:T(128)S(1)} %get-tuple-element.119) | copy-start | bytes 1540
  26.0 20.5 %copy-start.36 = (pred[128,128]{0,1:T(8,128)(4,1)}, pred[128,128]{0,1:T(8,128)(4,1)S(1)}, u32[]{:S(2)}) copy-start(pred[128,128]{0,1:T(8,128)(4,1)S(1)} %broadcast_compare_fusion) | copy-start | bytes 49156
  44.9 42.0 %copy-start.2 = (bf16[128,768]{0,1:T(8,128)(2,1)}, bf16[128,768]{0,1:T(8,128)(2,1)S(1)}, u32[]{:S(2)}) copy-start(bf16[128,768]{0,1:T(8,128)(2,1)S(1)} %copy.36) | copy-start | bytes 589828
  45.1 11.3 %copy-start.4 = (bf16[128,768]{0,1:T(8,128)(2,1)}, bf16[128,768]{0,1:T(8,128)(2,1)S(1)}, u32[]{:S(2)}) copy-start(bf16[128,768]{0,1:T(8,128)(2,1)S(1)} %copy.35) | copy-start | bytes 589828
  46.4 9.9 %copy-start.49 = (f32[8,128]{1,0:T(8,128)}, f32[8,128]{1,0:T(8,128)S(1)}, u32[]{:S(2)}) copy-start(f32[8,128]{1,0:T(8,128)S(1)} %get-tuple-element.142) | copy-start | bytes 12292
  47.0 11.6 %copy-start.1 = (bf16[128,1536]{1,0:T(8,128)(2,1)S(1)}, bf16[128,1536]{1,0:T(8,128)(2,1)}, u32[]{:S(2)}) copy-start(bf16[128,1536]{1,0:T(8,128)(2,1)} %param.12) | copy-start | bytes 1179652
  76.6 2.3 copy-start.26
  76.6 2.9 copy-start.25
  76.6 3.4 %copy-start.24 = (f32[1536]{0:T(1024)S(1)}, f32[1536]{0:T(1024)}, u32[]{:S(2)}) copy-start(f32[1536]{0:T(1024)} %get-tuple-element.7) | copy-start | bytes 18436
  76.6 4.0 %copy-start.23 = (f32[1536]{0:T(1024)S(1)}, f32[1536]{0:T(1024)}, u32[]{:S(2)}) copy-start(f32[1536]{0:T(1024)} %get-tuple-element.8) | copy-start | bytes 18436
  76.6 4.6 %copy-start.22 = (f32[1536]{0:T(1024)S(1)}, f32[1536]{0:T(1024)}, u32[]{:S(2)}) copy-start(f32[1536]{0:T(1024)} %get-tuple-element.9) | copy-start | bytes 18436
  76.6 5.2 %copy-start.21 = (f32[1536]{0:T(1024)S(1)}, f32[1536]{0:T(1024)}, u32[]{:S(2)}) copy-start(f32[1536]{0:T(1024)} %get-tuple-element.10) | copy-start | bytes 18436
  76.6 5.8 %copy-start.20 = (f32[1536]{0:T(1024)S(1)}, f32[1536]{0:T(1024)}, u32[]{:S(2)}) copy-start(f32[1536]{0:T(1024)} %get-tuple-element.11) | copy-start | bytes 18436
  76.6 6.4 %copy-start.19 = (f32[1536]{0:T(1024)S(1)}, f32[1536]{0:T(1024)}, u32[]{:S(2)}) copy-start(f32[1536]{0:T(1024)} %get-tuple-element.12) | copy-start | bytes 18436
  76.6 7.0 %copy-start.18 = (f32[1536]{0:T(1024)S(1)}, f32[1536]{0:T(1024)}, u32[]{:S(2)}) copy-start(f32[1536]{0:T(1024)} %get-tuple-element.13) | copy-start | bytes 18436
  78.8 8.2 %copy-start.5 = (bf16[128,768]{0,1:T(8,128)(2,1)S(1)}, bf16[128,768]{0,1:T(8,128)(2,1)}, u32[]{:S(2)}) copy-start(bf16[128,768]{0,1:T(8,128)(2,1)} %copy-done.4) | copy-start | bytes 589828
  88.3 2.3 copy-start.3
  88.3 2.3 copy-start.50
  95.7 14.0 %copy-start.13 = (f32[1536]{0:T(1024)S(1)}, f32[1536]{0:T(1024)}, u32[]{:S(2)}) copy-start(f32[1536]{0:T(1024)} %get-tuple-element.23) | copy-start | bytes 18436
  95.7 14.0 %copy-start.12 = (f32[1536]{0:T(1024)S(1)}, f32[1536]{0:T(1024)}, u32[]{:S(2)}) copy-start(f32[1536]{0:T(1024)} %get-tuple-element.24) | copy-start | bytes 18436
  95.7 14.0 %copy-start.11 = (f32[1536]{0:T(1024)S(1)}, f32[1536]{0:T(1024)}, u32[]{:S(2)}) copy-start(f32[1536]{0:T(1024)} %get-tuple-element.25) | copy-start | bytes 18436
  95.7 14.1 %copy-start.10 = (f32[1536]{0:T(1024)S(1)}, f32[1536]{0:T(1024)}, u32[]{:S(2)}) copy-start(f32[1536]{0:T(1024)} %get-tuple-element.26) | copy-start | bytes 18436
  95.7 14.1 %copy-start.9 = (f32[1536]{0:T(1024)S(1)}, f32[1536]{0:T(1024)}, u32[]{:S(2)}) copy-start(f32[1536]{0:T(1024)} %get-tuple-element.27) | copy-start | bytes 18436
  95.7 14.1 %copy-start.8 = (f32[1536]{0:T(1024)S(1)}, f32[1536]{0:T(1024)}, u32[]{:S(2)}) copy-start(f32[1536]{0:T(1024)} %get-tuple-element.28) | copy-start | bytes 18436
  95.7 14.1 %copy-start.7 = (f32[1536]{0:T(1024)S(1)}, f32[1536]{0:T(1024)}, u32[]{:S(2)}) copy-start(f32[1536]{0:T(1024)} %get-tuple-element.29) | copy-start | bytes 18436
  95.7 14.1 %copy-start.17 = (f32[1536]{0:T(1024)S(1)}, f32[1536]{0:T(1024)}, u32[]{:S(2)}) copy-start(f32[1536]{0:T(1024)} %get-tuple-element.32) | copy-start | bytes 18436
  95.7 14.2 %copy-start.16 = (f32[1536]{0:T(1024)S(1)}, f32[1536]{0:T(1024)}, u32[]{:S(2)}) copy-start(f32[1536]{0:T(1024)} %get-tuple-element.33) | copy-start | bytes 18436
  95.8 14.2 %copy-start.15 = (f32[1536]{0:T(1024)S(1)}, f32[1536]{0:T(1024)}, u32[]{:S(2)}) copy-start(f32[1536]{0:T(1024)} %get-tuple-element.34) | copy-start | bytes 18436
  95.8 14.2 %copy-start.14 = (f32[1536]{0:T(1024)S(1)}, f32[1536]{0:T(1024)}, u32[]{:S(2)}) copy-start(f32[1536]{0:T(1024)} %get-tuple-element.35) | copy-start | bytes 18436
  95.8 14.2 %copy-start.27 = (f32[1,1536]{1,0:T(1,128)S(1)}, f32[1,1536]{1,0:T(1,128)}, u32[]{:S(2)}) copy-start(f32[1,1536]{1,0:T(1,128)} %reshape.271) | copy-start | bytes 18436
  95.8 14.2 %copy-start.28 = (f32[1,1536]{1,0:T(1,128)S(1)}, f32[1,1536]{1,0:T(1,128)}, u32[]{:S(2)}) copy-start(f32[1,1536]{1,0:T(1,128)} %reshape.272) | copy-start | bytes 18436
  95.8 14.2 %copy-start.29 = (f32[1,1536]{1,0:T(1,128)S(1)}, f32[1,1536]{1,0:T(1,128)}, u32[]{:S(2)}) copy-start(f32[1,1536]{1,0:T(1,128)} %reshape.273) | copy-start | bytes 18436
  95.8 14.2 %copy-start.30 = (f32[1,1536]{1,0:T(1,128)S(1)}, f32[1,1536]{1,0:T(1,128)}, u32[]{:S(2)}) copy-start(f32[1,1536]{1,0:T(1,128)} %reshape.274) | copy-start | bytes 18436
  96.8 13.2 %copy-start.31 = (f32[1,1536]{1,0:T(1,128)S(1)}, f32[1,1536]{1,0:T(1,128)}, u32[]{:S(2)}) copy-start(f32[1,1536]{1,0:T(1,128)} %reshape.275) | copy-start | bytes 18436
  96.8 13.2 %copy-start.32 = (f32[1,1536]{1,0:T(1,128)S(1)}, f32[1,1536]{1,0:T(1,128)}, u32[]{:S(2)}) copy-start(f32[1,1536]{1,0:T(1,128)} %reshape.276) | copy-start | bytes 18436
  96.8 13.3 %copy-start.33 = (f32[1,1536]{1,0:T(1,128)S(1)}, f32[1,1536]{1,0:T(1,128)}, u32[]{:S(2)}) copy-start(f32[1,1536]{1,0:T(1,128)} %reshape.277) | copy-start | bytes 18436
  96.8 13.3 %copy-start.34 = (f32[1,1536]{1,0:T(1,128)S(1)}, f32[1,1536]{1,0:T(1,128)}, u32[]{:S(2)}) copy-start(f32[1,1536]{1,0:T(1,128)} %reshape.278) | copy-start | bytes 18436
  96.8 13.3 %copy-start.35 = (f32[1,1536]{1,0:T(1,128)S(1)}, f32[1,1536]{1,0:T(1,128)}, u32[]{:S(2)}) copy-start(f32[1,1536]{1,0:T(1,128)} %reshape.279) | copy-start | bytes 18436
  96.8 157.1 %all-to-all-start.1 = ((bf16[32,4,2304]{2,1,0:T(4,128)(2,1)}), bf16[32,4,2304]{2,1,0:T(4,128)(2,1)S(1)}, u32[]{:S(2)}, u32[]{:S(2)}) async-start(bf16[32,4,2304]{2,1,0:T(4,128)(2,1)} %all_to_all.25), calls=%async_computation.1 | async-start | bytes 1179648 | tf_op jit(solution)/shard_map/all_to_all | solution.py:119
  107.1 144.2 %all-reduce.66.cloned.1.call-start = ((), (), s32[]{:S(2)}) async-start(), calls=%async_computation.6 | async-start | bytes 393216 | tf_op jit(solution)/shard_map/psum | solution.py:123
  253.8 29.7 %all-to-all-start.2 = ((f32[32,1,4608]{2,1,0:T(1,128)}), f32[32,1,4608]{2,1,0:T(1,128)S(1)}, u32[]{:S(2)}, u32[]{:S(2)}) async-start(f32[32,1,4608]{2,1,0:T(1,128)} %all_to_all.30), calls=%async_computation.3 | async-start | bytes 1179648 | tf_op jit(solution)/shard_map/all_to_all | solution.py:146
Sparse Core Ops, SparseCore 0:
  10.1 46.2 all-gather.3
  78.9 58.4 reduce-scatter.1
  140.4 110.8 all-reduce.65
where the time goes:
time: 342 us
  waiting for transfers between devices  184 us (54%)
  blocking collectives  48.8 us (14%)
  starting transfers between devices  33.8 us (10%)
  other arithmetic  28.4 us (8%)
  local copies, waits for them, and re-layouts  17.9 us (5%)
  between operations  14.9 us (4%)
  matrix products  14 us (4%)
    psum x1, waiting for transfers between devices, body(): kernel_f = lax.psum(kernel_part, 'fsdp')  113 us
    all_gather x1, blocking collectives, dp_allreduce_a2a(): return lax.all_gather(part, 'dp', axis=0, tiled=True).reshape(x.shape)  48.8 us
    reduce_scatter x1, waiting for transfers between devices, body(): lax.psum_scatter(jnp.einsum('rc,rd->cd', columns, mixed_grad, preferred_e...  26.3 us
    all_to_all x1, waiting for transfers between devices, body(): lax.all_to_all(outgoing, 'dp', split_axis=0, concat_axis=0, tiled=True)  17.5 us
    all_to_all x1, waiting for transfers between devices, dp_allreduce_a2a(): got = lax.all_to_all(flat, 'dp', split_axis=0, concat_axis=0, tiled=True)  17 us
    reduce_sum x4, other arithmetic, finish(): kernel[offset] * padded[offset:offset + length] * matching[:, None]  14.9 us
    all_to_all x1, starting transfers between devices, body(): lax.all_to_all(outgoing, 'dp', split_axis=0, concat_axis=0, tiled=True)  13.2 us
    all_to_all x1, starting transfers between devices, body(): lax.all_to_all(returning, 'dp', split_axis=0, concat_axis=0, tiled=True)  10.3 us
  transfers between devices with their start and end apart: 6, of which 5 were waited for; matrix products, arithmetic and copies ran while one was open for 9% of the time, Pallas kernels for 0%

commit v1 on v0

--- a/solution.py
+++ b/solution.py
@@ -5,6 +5,11 @@
 
 HEADS = 8
 HEAD_DIM = 96
+
+
+def gather_over(array, axis, dim):
+    repeated = jnp.stack([array] * lax.axis_size(axis))
+    return jnp.concatenate(lax.all_to_all(repeated, axis, 0, 0), axis=dim)
 
 
 def split_heads(frames):
@@ -88,9 +93,7 @@
     context, soft_probs, rounded = attend(frames, segment)
     columns = context
     mixed_sums = jnp.dot(
-        columns,
-        lax.all_gather(out_weight, "fsdp", axis=0, tiled=True),
-        preferred_element_type=jnp.float32,
+        columns, gather_over(out_weight, "fsdp", 0), preferred_element_type=jnp.float32
     )
     mixed = mixed_sums.astype(jnp.bfloat16)
     result, pullback = jax.vjp(

time: 342 us -> 396 us (1.16)
  waiting for transfers between devices: 184 us -> 221 us
  blocking collectives: 48.8 us -> 80.8 us
  starting transfers between devices: 33.8 us -> 21.9 us
  local copies, waits for them, and re-layouts: 17.9 us -> 13.3 us
    all_to_all x1, waiting for transfers between devices: 17.5 us -> 58.3 us  [gather_over(): return jnp.concatenate(lax.all_to_all(repeated, axis, 0, 0), axis=dim)]
    all_to_all x0 -> x1, blocking collectives: none -> 32 us  [body(): lax.all_to_all(outgoing, 'dp', split_axis=0, concat_axis=0, tiled=True)]
    all_gather x1, waiting for transfers between devices: 9.41 us -> 0.02 us  [body(): lax.all_gather(out_weight, 'fsdp', axis=0, tiled=True)]
    reduce_scatter x1, waiting for transfers between devices: 26.3 us -> 32.8 us  [body(): lax.psum_scatter(jnp.einsum('rc,rd->cd', columns, mixed_grad, preferred_e...]
    all_to_all x1, starting transfers between devices: 10.3 us -> 4.18 us  [body(): lax.all_to_all(returning, 'dp', split_axis=0, concat_axis=0, tiled=True)]
    all_to_all x1, starting transfers between devices: 13.2 us -> 7.47 us  [gather_over(): return jnp.concatenate(lax.all_to_all(repeated, axis, 0, 0), axis=dim)]
    reshape x31, local copies, waits for them, and re-layouts: 5.52 us -> 0.2 us  [finish(): kernel[offset] * padded[offset:offset + length] * matching[:, None]]
  transfers between devices with their start and end apart: 6 -> 6, of which waited for: 5 -> 4; matrix products, arithmetic and copies ran while one was open for 9% -> 12% of each run, Pallas kernels for 0% -> 0%
where the time goes in v1:
time: 396 us; the launch traced here: 395 us
  waiting for transfers between devices  221 us (56%)
  blocking collectives  80.8 us (20%)
  other arithmetic  29.1 us (7%)
  starting transfers between devices  21.9 us (6%)
  between operations  14.9 us (4%)
  matrix products  14.1 us (4%)
  local copies, waits for them, and re-layouts  13.3 us (3%)
    psum x1, waiting for transfers between devices, body(): kernel_f = lax.psum(kernel_part, 'fsdp')  113 us
    all_to_all x1, waiting for transfers between devices, gather_over(): return jnp.concatenate(lax.all_to_all(repeated, axis, 0, 0), axis=dim)  58.3 us
    all_gather x1, blocking collectives, dp_allreduce_a2a(): return lax.all_gather(part, 'dp', axis=0, tiled=True).reshape(x.shape)  48.8 us
    reduce_scatter x1, waiting for transfers between devices, body(): lax.psum_scatter(jnp.einsum('rc,rd->cd', columns, mixed_grad, preferred_e...  32.8 us
    all_to_all x1, blocking collectives, body(): lax.all_to_all(outgoing, 'dp', split_axis=0, concat_axis=0, tiled=True)  32 us
    all_to_all x1, waiting for transfers between devices, dp_allreduce_a2a(): got = lax.all_to_all(flat, 'dp', split_axis=0, concat_axis=0, tiled=True)  17 us
    reduce_sum x4, other arithmetic, finish(): kernel[offset] * padded[offset:offset + length] * matching[:, None]  14.8 us
    all_to_all x1, starting transfers between devices, dp_allreduce_a2a(): got = lax.all_to_all(flat, 'dp', split_axis=0, concat_axis=0, tiled=True)  10.2 us
  transfers between devices with their start and end apart: 6, of which 4 were waited for; matrix products, arithmetic and copies ran while one was open for 12% of the time, Pallas kernels for 0%

profile of v1, /device:TPU:24, one launch (start us, length us, event | category | flops | bytes accessed | tf_op | source)
XLA Modules:
  0.0 395.5 jit_solution(7598536106117692705)
XLA Ops:
  7.2 1.3 compare_select_fusion.1
  8.4 0.7 broadcast_compare_fusion.3
  9.1 1.0 gather_fusion
  10.1 0.2 select_select_fusion.1
  10.3 0.1 all_to_all.25
  10.4 32.0 %all_to_all.39 = bf16[32,4,2304]{2,1,0:T(4,128)(2,1)S(1)} all-to-all(bf16[32,4,2304]{2,1,0:T(4,128)(2,1)S(1)} %all_to_all.25), channel_id=1, replica_groups=mesh['dp'=32,'fsdp'=16] {'dp'}, dimensions={0} | all-to-all | bytes 1179648 | tf_op jit(solution)/shard_map/all_to_all | solution.py:89
  42.4 1.7 stack.2
  44.1 7.5 %all-to-all-start.1 = ((bf16[16,48,1536]{2,1,0:T(8,128)(2,1)}), bf16[16,48,1536]{2,1,0:T(8,128)(2,1)}, u32[]{:S(2)}, u32[]{:S(2)}) async-start(bf16[16,48,1536]{2,1,0:T(8,128)(2,1)} %stack.2), calls=%async_computation.1 | async-start | bytes 4718592 | tf_op jit(solution)/shard_map/all_to_all | solution.py:12
  51.6 0.7 all-gather.4.cloned.1.call-update
  52.3 0.5 compare_select_fusion
  52.8 0.2 slice_reduce_fusion.29
  53.0 0.3 slice_reduce_fusion.30
  53.4 0.1 compare_convert_fusion.28
  53.5 0.1 compare_convert_fusion.29
  53.7 0.1 broadcast_compare_fusion
  53.8 0.1 all_to_all.27
  53.9 1.0 gather_fusion.1
  54.9 0.2 select_select_fusion
  55.1 0.2 copy.35
  55.3 0.2 copy.36
  55.4 0.2 copy.34
  55.6 1.2 fusion.40
  56.8 0.5 convolution_convert_fusion.6
  57.3 58.3 %all-to-all-done.1 = bf16[16,48,1536]{2,1,0:T(8,128)(2,1)} async-done(((bf16[16,48,1536]{2,1,0:T(8,128)(2,1)}), bf16[16,48,1536]{2,1,0:T(8,128)(2,1)}, u32[]{:S(2)}, u32[]{:S(2)}) %all-to-all-start.1) | async-done | bytes 2359328 | tf_op jit(solution)/shard_map/all_to_all | solution.py:12
  115.6 2.2 fusion.2
  117.8 7.6 %multiply_reduce_fusion.31 = (f32[1536]{0:T(1024)}, f32[1536]{0:T(1024)}, f32[1536]{0:T(1024)}, f32[1536]{0:T(1024)}, f32[1536]{0:T(1024)}, /*index=5*/f32[1536]...) fusion(f32[128,1536]{1,0:T(8,128)S(1)} %fusion.2, ...), kind=kLoop, calls=%fused_computation.99 | loop fusion | flops 25152000 | bytes 3013632 | tf_op jit(solution)/shard_map/transpose(jvp())/reduce_sum | solution.py:79
  125.4 2.3 multiply_reduce_fusion.16
  127.7 2.6 multiply_reduce_fusion.4
  130.3 0.5 multiply_multiply_fusion.27
  130.9 0.7 multiply_multiply_fusion.28
  131.6 0.7 multiply_multiply_fusion.29
  132.4 2.8 pad_add_fusion
  135.2 0.7 fusion.16
  135.8 2.2 convolution_convert_fusion
  138.1 2.5 convolution_convert_fusion.5
  140.6 0.2 copy.38
  140.8 0.3 fusion.41
  141.1 1.6 convolution_convert_fusion.4
  142.7 0.1 copy.42
  142.8 2.2 convolution_convert_fusion.3
  145.0 1.1 copy.43
  146.1 1.5 convolution_convert_fusion.2
  147.6 0.1 copy.44
  147.7 1.8 scatter_custom_fusion
  149.7 1.0 all_to_all.29
  150.6 4.2 %all-to-all-start.2 = ((bf16[32,4,2304]{2,1,0:T(4,128)(2,1)}), bf16[32,4,2304]{2,1,0:T(4,128)(2,1)S(1)}, u32[]{:S(2)}, u32[]{:S(2)}) async-start(bf16[32,4,2304]{2,1,0:T(4,128)(2,1)} %all_to_all.29), calls=%async_computation.2 | async-start | bytes 1179648 | tf_op jit(solution)/shard_map/all_to_all | solution.py:122
  154.8 0.0 all-reduce.66.cloned.1.call-start
  154.9 2.3 multiply_reduce_fusion.22
  157.9 1.0 pad_add_fusion.7
  158.9 0.1 pad.266.clone
  159.0 32.8 %reduce-scatter.2.cloned.1.call-done = bf16[48,1536]{1,0:T(8,128)(2,1)} async-done(((bf16[768,1536]{1,0:T(8,128)(2,1)}), bf16[48,1536]{1,0:T(8,128)(2,1)}) %reduce-scatter.2.cloned.1.call-update) | async-done | bytes 147472 | tf_op jit(solution)/shard_map/reduce_scatter | solution.py:104
  191.8 0.9 convert_element_type.214
  192.7 112.5 %all-reduce.66.cloned.1.call-done = f32[31,1536]{1,0:T(8,128)} async-done(((f32[31,1536]{1,0:T(8,128)}), f32[31,1536]{1,0:T(8,128)}) %all-reduce.66.cloned.1.call-update) | async-done | bytes 190480 | tf_op jit(solution)/shard_map/psum | solution.py:126
  305.2 1.0 maximum_maximum_fusion
  306.3 1.5 all_to_all.34
  307.8 10.2 %all-to-all-start.3 = ((f32[32,1,4608]{2,1,0:T(1,128)}), f32[32,1,4608]{2,1,0:T(1,128)S(1)}, u32[]{:S(2)}, u32[]{:S(2)}) async-start(f32[32,1,4608]{2,1,0:T(1,128)} %all_to_all.34), calls=%async_computation.4 | async-start | bytes 1179648 | tf_op jit(solution)/shard_map/all_to_all | solution.py:149
  318.0 0.1 reshape.338
  318.1 2.4 scatter_custom_fusion.1
  320.5 17.0 %all-to-all-done.3 = f32[32,1,4608]{2,1,0:T(1,128)S(1)} async-done(((f32[32,1,4608]{2,1,0:T(1,128)}), f32[32,1,4608]{2,1,0:T(1,128)S(1)}, u32[]{:S(2)}, u32[]{:S(2)}) %all-to-all-start.3) | async-done | bytes 589856 | tf_op jit(solution)/shard_map/all_to_all | solution.py:149
  337.5 0.3 reduce_sum.356
  337.8 48.8 %all-gather.1 = f32[32,1,4608]{2,1,0:T(1,128)S(1)} all-gather(f32[1,1,4608]{2,1,0:T(1,128)S(1)} %reshape.355), channel_id=2, replica_groups=mesh['dp'=32,'fsdp'=16] {'dp'}, dimensions={0}, use_global_device_ids=true | all-gather | bytes 608256 | tf_op jit(solution)/shard_map/all_gather | solution.py:151
  386.7 0.8 fusion.23
  387.5 0.8 mul.1323
  388.3 0.7 reshape.353
  (124 shorter events, 0.6 us)
Async XLA Ops:
  7.2 1.9 copy-start
  10.1 32.3 %copy-start.2 = (bf16[48,1536]{1,0:T(8,128)(2,1)S(1)}, bf16[48,1536]{1,0:T(8,128)(2,1)}, u32[]{:S(2)}) copy-start(bf16[48,1536]{1,0:T(8,128)(2,1)} %param.10) | copy-start | bytes 442372
  44.1 8.3 %copy-start.37 = (s32[128]{0:T(128)S(1)}, s32[128]{0:T(128)}, u32[]{:S(2)}) copy-start(s32[128]{0:T(128)} %param.14) | copy-start | bytes 1540
  44.1 8.8 %copy-start.6 = (f32[31,1536]{1,0:T(8,128)S(1)}, f32[31,1536]{1,0:T(8,128)}, u32[]{:S(2)}) copy-start(f32[31,1536]{1,0:T(8,128)} %param.11) | copy-start | bytes 571396
  44.1 9.3 %copy-start.36 = (s32[128]{0:T(128)S(1)}, s32[128]{0:T(128)}, u32[]{:S(2)}) copy-start(s32[128]{0:T(128)} %param.15) | copy-start | bytes 1540
  44.1 71.6 %all-to-all-start.1 = ((bf16[16,48,1536]{2,1,0:T(8,128)(2,1)}), bf16[16,48,1536]{2,1,0:T(8,128)(2,1)}, u32[]{:S(2)}, u32[]{:S(2)}) async-start(bf16[16,48,1536]{2,1,0:T(8,128)(2,1)} %stack.2), calls=%async_computation.1 | async-start | bytes 4718592 | tf_op jit(solution)/shard_map/all_to_all | solution.py:12
  51.5 86.5 %all-gather.4.cloned.1.call-start = ((), (), s32[]{:S(2)}) async-start(), calls=%async_computation.5 | async-start | bytes 2506752 | tf_op jit(solution)/shard_map/all_gather | solution.py:115
  52.3 139.5 %reduce-scatter.2.cloned.1.call-start = ((), (), s32[]{:S(2)}) async-start(), calls=%async_computation.6 | async-start | bytes 2506752 | tf_op jit(solution)/shard_map/reduce_scatter | solution.py:104
  53.6 77.2 %copy-start.27 = (f32[128]{0:T(128)}, f32[128]{0:T(128)S(1)}, u32[]{:S(2)}) copy-start(f32[128]{0:T(128)S(1)} %get-tuple-element.114) | copy-start | bytes 1540
  53.6 77.2 %copy-start.28 = (f32[128]{0:T(128)}, f32[128]{0:T(128)S(1)}, u32[]{:S(2)}) copy-start(f32[128]{0:T(128)S(1)} %get-tuple-element.115) | copy-start | bytes 1540
  53.6 77.2 %copy-start.29 = (f32[128]{0:T(128)}, f32[128]{0:T(128)S(1)}, u32[]{:S(2)}) copy-start(f32[128]{0:T(128)S(1)} %get-tuple-element.116) | copy-start | bytes 1540
  53.6 77.2 %copy-start.30 = (f32[128]{0:T(128)}, f32[128]{0:T(128)S(1)}, u32[]{:S(2)}) copy-start(f32[128]{0:T(128)S(1)} %get-tuple-element.117) | copy-start | bytes 1540
  53.6 77.2 %copy-start.31 = (f32[128]{0:T(128)}, f32[128]{0:T(128)S(1)}, u32[]{:S(2)}) copy-start(f32[128]{0:T(128)S(1)} %get-tuple-element.118) | copy-start | bytes 1540
  53.6 77.2 %copy-start.32 = (f32[128]{0:T(128)}, f32[128]{0:T(128)S(1)}, u32[]{:S(2)}) copy-start(f32[128]{0:T(128)S(1)} %get-tuple-element.119) | copy-start | bytes 1540
  53.6 77.9 %copy-start.33 = (f32[128]{0:T(128)}, f32[128]{0:T(128)S(1)}, u32[]{:S(2)}) copy-start(f32[128]{0:T(128)S(1)} %get-tuple-element.120) | copy-start | bytes 1540
  53.7 77.9 %copy-start.34 = (f32[128]{0:T(128)}, f32[128]{0:T(128)S(1)}, u32[]{:S(2)}) copy-start(f32[128]{0:T(128)S(1)} %get-tuple-element.121) | copy-start | bytes 1540
  53.7 77.9 %copy-start.35 = (f32[128]{0:T(128)}, f32[128]{0:T(128)S(1)}, u32[]{:S(2)}) copy-start(f32[128]{0:T(128)S(1)} %get-tuple-element.122) | copy-start | bytes 1540
  55.2 2.0 copy-start.3
  55.4 60.2 %copy-start.5 = (bf16[128,768]{0,1:T(8,128)(2,1)}, bf16[128,768]{0,1:T(8,128)(2,1)S(1)}, u32[]{:S(2)}) copy-start(bf16[128,768]{0,1:T(8,128)(2,1)S(1)} %copy.36) | copy-start | bytes 589828
  56.8 61.1 %copy-start.38 = (f32[8,128]{1,0:T(8,128)}, f32[8,128]{1,0:T(8,128)S(1)}, u32[]{:S(2)}) copy-start(f32[8,128]{1,0:T(8,128)S(1)} %get-tuple-element.142) | copy-start | bytes 12292
  57.3 60.5 %copy-start.1 = (bf16[128,1536]{1,0:T(8,128)(2,1)S(1)}, bf16[128,1536]{1,0:T(8,128)(2,1)}, u32[]{:S(2)}) copy-start(bf16[128,1536]{1,0:T(8,128)(2,1)} %param.12) | copy-start | bytes 1179652
  138.0 3.0 copy-start.39
  140.6 2.2 copy-start.4
  149.5 7.9 %copy-start.26 = (f32[1536]{0:T(1024)S(1)}, f32[1536]{0:T(1024)}, u32[]{:S(2)}) copy-start(f32[1536]{0:T(1024)} %get-tuple-element.23) | copy-start | bytes 18436
  149.5 7.9 %copy-start.24 = (f32[1536]{0:T(1024)S(1)}, f32[1536]{0:T(1024)}, u32[]{:S(2)}) copy-start(f32[1536]{0:T(1024)} %get-tuple-element.24) | copy-start | bytes 18436
  149.5 7.9 %copy-start.22 = (f32[1536]{0:T(1024)S(1)}, f32[1536]{0:T(1024)}, u32[]{:S(2)}) copy-start(f32[1536]{0:T(1024)} %get-tuple-element.25) | copy-start | bytes 18436
  149.5 7.9 %copy-start.20 = (f32[1536]{0:T(1024)S(1)}, f32[1536]{0:T(1024)}, u32[]{:S(2)}) copy-start(f32[1536]{0:T(1024)} %get-tuple-element.26) | copy-start | bytes 18436
  149.5 7.9 %copy-start.18 = (f32[1536]{0:T(1024)S(1)}, f32[1536]{0:T(1024)}, u32[]{:S(2)}) copy-start(f32[1536]{0:T(1024)} %get-tuple-element.27) | copy-start | bytes 18436
  149.5 7.9 %copy-start.17 = (f32[1536]{0:T(1024)S(1)}, f32[1536]{0:T(1024)}, u32[]{:S(2)}) copy-start(f32[1536]{0:T(1024)} %get-tuple-element.28) | copy-start | bytes 18436
  149.6 7.9 %copy-start.16 = (f32[1536]{0:T(1024)S(1)}, f32[1536]{0:T(1024)}, u32[]{:S(2)}) copy-start(f32[1536]{0:T(1024)} %get-tuple-element.29) | copy-start | bytes 18436
  149.6 8.0 %copy-start.15 = (f32[1536]{0:T(1024)S(1)}, f32[1536]{0:T(1024)}, u32[]{:S(2)}) copy-start(f32[1536]{0:T(1024)} %get-tuple-element.30) | copy-start | bytes 18436
  149.6 8.0 %copy-start.14 = (f32[1536]{0:T(1024)S(1)}, f32[1536]{0:T(1024)}, u32[]{:S(2)}) copy-start(f32[1536]{0:T(1024)} %get-tuple-element.31) | copy-start | bytes 18436
  149.6 8.0 %copy-start.25 = (f32[1536]{0:T(1024)S(1)}, f32[1536]{0:T(1024)}, u32[]{:S(2)}) copy-start(f32[1536]{0:T(1024)} %get-tuple-element.32) | copy-start | bytes 18436
  149.6 8.0 %copy-start.23 = (f32[1536]{0:T(1024)S(1)}, f32[1536]{0:T(1024)}, u32[]{:S(2)}) copy-start(f32[1536]{0:T(1024)} %get-tuple-element.33) | copy-start | bytes 18436
  149.6 8.0 %copy-start.21 = (f32[1536]{0:T(1024)S(1)}, f32[1536]{0:T(1024)}, u32[]{:S(2)}) copy-start(f32[1536]{0:T(1024)} %get-tuple-element.34) | copy-start | bytes 18436
  149.6 8.0 %copy-start.19 = (f32[1536]{0:T(1024)S(1)}, f32[1536]{0:T(1024)}, u32[]{:S(2)}) copy-start(f32[1536]{0:T(1024)} %get-tuple-element.35) | copy-start | bytes 18436
  149.6 8.0 %copy-start.13 = (f32[1536]{0:T(1024)S(1)}, f32[1536]{0:T(1024)}, u32[]{:S(2)}) copy-start(f32[1536]{0:T(1024)} %get-tuple-element.5) | copy-start | bytes 18436
  149.6 8.1 %copy-start.12 = (f32[1536]{0:T(1024)S(1)}, f32[1536]{0:T(1024)}, u32[]{:S(2)}) copy-start(f32[1536]{0:T(1024)} %get-tuple-element.6) | copy-start | bytes 18436
  149.6 8.1 %copy-start.11 = (f32[1536]{0:T(1024)S(1)}, f32[1536]{0:T(1024)}, u32[]{:S(2)}) copy-start(f32[1536]{0:T(1024)} %get-tuple-element.7) | copy-start | bytes 18436
  149.7 8.1 %copy-start.10 = (f32[1536]{0:T(1024)S(1)}, f32[1536]{0:T(1024)}, u32[]{:S(2)}) copy-start(f32[1536]{0:T(1024)} %get-tuple-element.8) | copy-start | bytes 18436
  149.7 8.1 %copy-start.9 = (f32[1536]{0:T(1024)S(1)}, f32[1536]{0:T(1024)}, u32[]{:S(2)}) copy-start(f32[1536]{0:T(1024)} %get-tuple-element.9) | copy-start | bytes 18436
  149.7 8.1 %copy-start.8 = (f32[1536]{0:T(1024)S(1)}, f32[1536]{0:T(1024)}, u32[]{:S(2)}) copy-start(f32[1536]{0:T(1024)} %get-tuple-element.10) | copy-start | bytes 18436
  149.7 8.1 %copy-start.7 = (f32[1536]{0:T(1024)S(1)}, f32[1536]{0:T(1024)}, u32[]{:S(2)}) copy-start(f32[1536]{0:T(1024)} %get-tuple-element.11) | copy-start | bytes 18436
  150.6 157.1 %all-to-all-start.2 = ((bf16[32,4,2304]{2,1,0:T(4,128)(2,1)}), bf16[32,4,2304]{2,1,0:T(4,128)(2,1)S(1)}, u32[]{:S(2)}, u32[]{:S(2)}) async-start(bf16[32,4,2304]{2,1,0:T(4,128)(2,1)} %all_to_all.29), calls=%async_computation.2 | async-start | bytes 1179648 | tf_op jit(solution)/shard_map/all_to_all | solution.py:122
  154.8 150.4 %all-reduce.66.cloned.1.call-start = ((), (), s32[]{:S(2)}) async-start(), calls=%async_computation.7 | async-start | bytes 393216 | tf_op jit(solution)/shard_map/psum | solution.py:126
  307.8 29.7 %all-to-all-start.3 = ((f32[32,1,4608]{2,1,0:T(1,128)}), f32[32,1,4608]{2,1,0:T(1,128)S(1)}, u32[]{:S(2)}, u32[]{:S(2)}) async-start(f32[32,1,4608]{2,1,0:T(1,128)} %all_to_all.34), calls=%async_computation.4 | async-start | bytes 1179648 | tf_op jit(solution)/shard_map/all_to_all | solution.py:149
Sparse Core Ops, SparseCore 0:
  54.5 65.3 all-gather.3
  138.1 53.5 reduce-scatter.1
  194.7 110.4 all-reduce.65
